TPU v7x, 32 devices: a whole 2x2x4 slice. The times are simulated.
32 devices in a mesh: freq: 4 (over y, core), row: 8 (over z, x).
Axes of the slice: x: 2, y: 2, z: 4, core: 2. Of those that a mesh axis runs over, the one named last changes fastest.
Arguments:
- traces: bfloat16 [2, 8192, 8192], P(None, ('freq', 'row')), may hold values from -1.1953125 to 1.1953125
- prior: bfloat16 [4, 2, 8192, 8192], P('freq', None, None, 'row'), may hold values from -0.796875 to 0.796875
- bins: int32 [4], replicated, may hold values from 64 to 255
- panels: int32 [2], replicated, may hold values from 0 to 31
Outputs:
- multiples: bfloat16 [4, 2, 8192, 8192], P('freq', None, 'row')
- spectrum: bfloat16 [4, 2, 8192, 8192], P('freq', None, None, 'row')
All inputs are finite; a program needn't handle non-finite values.
Results may differ from a plain program's by a relative error of at most 0.0077.
Values may be sent and summed in bfloat16 or wider, within the bound.
No kernel may reach another device: no remote copies, remote signals or barrier semaphores. Data moves between devices by JAX's collectives and lax.ppermute only.
A program may use at most 640 MiB of HBM per device.

v0:
```python
import math
import jax
import jax.numpy as jnp
from jax import lax
from jax.sharding import PartitionSpec as P

NT_REC = 1024
PANEL = 256
STEPS = 2
BLOCK_START = 1022


def spread(value, axis, source):
    kept = jnp.where(lax.axis_index(axis) == source, value, 0).astype(value.dtype)
    return lax.psum(kept, axis)


def complex_terms(left, right):
    dims = (((0,), (1,)), ((), ()))

    def product(first, second):
        return lax.dot_general(first, second, dims, preferred_element_type=jnp.float32)

    real_part = product(left[0], right[0]) - product(left[1], right[1])
    imag_part = product(left[0], right[1]) + product(left[1], right[0])
    return (real_part, imag_part)


def body(traces, prior, bins, panels):
    sample_count, shots_local, receivers = traces.shape
    row_count = lax.axis_size("row")
    block_rows = receivers // row_count
    sample_index = BLOCK_START + jnp.arange(sample_count, dtype=jnp.int32)
    turn_count = bins[:, None] * sample_index[None, :] % NT_REC
    angles = 2.0 * math.pi / NT_REC * turn_count.astype(jnp.float32)
    twiddle = jnp.stack([jnp.cos(angles), -jnp.sin(angles)], axis=1).astype(jnp.bfloat16)
    own_twiddle = lax.dynamic_index_in_dim(twiddle, lax.axis_index("freq"), 0, keepdims=False)
    by_row = lax.all_to_all(traces, "row", split_axis=2, concat_axis=1, tiled=True)
    gathered = lax.all_gather(by_row, "freq", axis=1, tiled=True)
    transformed = jnp.einsum(
        "tsb,ct->csb", gathered, own_twiddle, preferred_element_type=jnp.float32
    ).astype(jnp.bfloat16)
    spectrum = (prior[0].astype(jnp.float32) + transformed.astype(jnp.float32)).astype(jnp.bfloat16)
    panels_each = block_rows // PANEL
    real_sum = jnp.zeros((block_rows, receivers), jnp.float32)
    imag_sum = jnp.zeros((block_rows, receivers), jnp.float32)
    for panel_step in range(STEPS):
        chosen = panels[panel_step]
        owner = chosen // panels_each
        offset = chosen % panels_each * PANEL
        own_rows = lax.dynamic_slice_in_dim(spectrum, offset, PANEL, 2)
        panel_data = spread(own_rows, "row", owner)
        left = lax.dynamic_slice_in_dim(spectrum, chosen * PANEL, PANEL, 1)
        real_part, imag_part = complex_terms(left, panel_data)
        real_sum = real_sum + real_part
        imag_sum = imag_sum + imag_part
    return (jnp.stack([real_sum, imag_sum])[None].astype(jnp.bfloat16), spectrum[None])


def solution(mesh):
    return jax.shard_map(
        body,
        mesh=mesh,
        in_specs=(P(None, ("freq", "row"), None), P("freq", None, None, "row"), P(), P()),
        out_specs=(P("freq", None, "row", None), P("freq", None, None, "row")),
        check_vma=False,
    )
```

profile of v0, /device:TPU:0, one launch (start us, length us, event | category | flops | bytes accessed | tf_op | source)
XLA Modules:
  0.0 1370.1 jit_solution(301745803882222178)
XLA Ops:
  7.2 0.0 all-gather.2.cloned.1.call-start
  7.2 21.0 %copy.21 = bf16[2,256,8192]{1,0,2:T(2,128)(2,1)} copy(bf16[2,256,8192]{2,1,0:T(8,128)(2,1)} %param.4) | data formatting | bytes 16777216 | tf_op args[0]
  28.2 190.4 %all_to_all.18 = bf16[2,256,8192]{1,0,2:T(2,128)(2,1)} all-to-all(bf16[2,256,8192]{1,0,2:T(2,128)(2,1)} %copy.21), channel_id=1, replica_groups=mesh['freq'=4,'row'=8] {'row'}, dimensions={2} | all-to-all | bytes 16777216 | tf_op jit(solution)/shard_map/all_to_all | solution.py:38
  218.6 30.5 %copy.22 = bf16[2,8,256,1024]{3,0,2,1:T(2,128)(2,1)} copy(bf16[2,8,256,1024]{2,0,3,1:T(2,128)(2,1)} %bitcast.60) | data formatting | bytes 16777216 | tf_op jit(solution)/shard_map/all_to_all | solution.py:38
  249.1 0.0 copy-start.1
  249.1 0.0 copy-start.2
  249.1 0.0 all-gather.2.cloned.1.call-update
  249.1 0.0 all-reduce.3.cloned.1.call-start
  249.2 0.6 copy-done.1
  249.8 0.6 fusion.49
  255.3 0.0 copy-done.2
  255.3 0.1 cosine_convert_fusion
  255.4 0.2 fusion.45
  255.6 194.4 %all-gather.2.cloned.1.call-done = bf16[2,8192,1024]{2,0,1:T(2,128)(2,1)} async-done(((bf16[2,2048,1024]{2,0,1:T(2,128)(2,1)}), bf16[2,8192,1024]{2,0,1:T(2,128)(2,1)}) %all-gather.2.cloned.1.call-update) | async-done | bytes 33554448 | tf_op jit(solution)/shard_map/all_gather | solution.py:39
  449.9 145.3 %fusion = bf16[2,8192,1024]{2,0,1:T(2,128)(2,1)} fusion(bf16[1,2,8192,1024]{3,2,1,0:T(8,128)(2,1)} %param.5, bf16[2,8192,1024]{2,0,1:T(2,128)(2,1)} %all-gather.2.cloned.1.call-done, bf16[2,2]{1,0:T(2,128)(2,1)S(1)} %fusion.45), kind=kOutput, calls=%fused_computation.1 | convolution fusion | flops 150994944 | bytes 100663304 | tf_op jit(solution)/shard_map/tsb,ct->csb/dot_general | solution.py:40
  595.3 17.1 %broadcast_select_fusion.1 = (bf16[2,8192,256]{2,0,1:T(2,128)(2,1)}, bf16[2,8192,256]{2,0,1:T(2,128)(2,1)}) fusion(pred[]{:T(512)S(6)} %eq.11, bf16[2,8192,1024]{2,0,1:T(2,128)(2,1)} %fusion, s32[]{:T(128)S(6)} %select_n.71, s32[]{:T(128)S(6)} %select_n.77, pred[]{:T(512)S(6)} %eq.12), kind=kLoop, calls=%fused_computation.7 | loop fusion | flops 8388608 | bytes 33554440 | tf_op jit(solution)/shard_map/jit(_where)/select_n | solution.py:14
  612.3 0.0 all-reduce.3.cloned.1.call-update
  613.6 23.4 %copy.23 = bf16[1,2,8192,1024]{3,2,1,0:T(8,128)(2,1)} copy(bf16[1,2,8192,1024]{3,1,2,0:T(2,128)(2,1)} %bitcast.58) | data formatting | bytes 67108864
  637.0 6.3 constant_dynamic-slice_fusion.3
  643.3 479.6 %all-reduce.3.cloned.1.call-done = (bf16[2,8192,256]{2,0,1:T(2,128)(2,1)}, bf16[2,8192,256]{2,0,1:T(2,128)(2,1)}) async-done(((bf16[2,8192,256]{2,0,1:T(2,128)(2,1)}, bf16[2,8192,256]{2,0,1:T(2,128)(2,1)}), (bf16[2,8192,256]{2,0,1:T(2,128)(2,1)}, bf16[2,8192,256]{2,0,1:T(2,128)(2,1)})) %all-reduce.3.cloned.1.call-update) | async-done | bytes 16777232 | tf_op jit(solution)/shard_map/psum | solution.py:15
  1122.9 33.0 %fusion.47 = (bf16[1,8192,256]{2,0,1:T(2,128)(2,1)}, bf16[1,8192,256]{2,0,1:T(2,128)(2,1)}, bf16[1,8192,256]{2,0,1:T(2,128)(2,1)}, bf16[1,8192,256]{2,0,1:T(2,128)(2,1)}) fusion(bf16[2,8192,256]{2,0,1:T(2,128)(2,1)} %get-tuple-element.12, bf16[2,8192,256]{2,0,1:T(2,128)(2,1)} %get-tuple-element.13), kind=kLoop, calls=%fused_computation.67 | loop fusion | bytes 33554432 | tf_op jit(solution)/shard_map/slice | solution.py:24
  1155.9 0.0 copy-start
  1155.9 19.5 %fusion.11 = f32[1024,8192]{1,0:T(8,128)} fusion(bf16[1,8192,256]{2,0,1:T(2,128)(2,1)} %get-tuple-element.28, bf16[1,256,1024]{2,0,1:T(2,128)(2,1)} %get-tuple-element.17), kind=kOutput, calls=%fused_computation.18 | convolution fusion | flops 4294967296 | bytes 38273024 | tf_op jit(solution)/shard_map/dot_general | solution.py:22
  1175.3 0.0 copy-done
  1175.3 16.5 %fusion.13 = f32[1024,8192]{1,0:T(8,128)} fusion(bf16[1,8192,256]{2,0,1:T(2,128)(2,1)} %get-tuple-element.29, bf16[1,256,1024]{2,0,1:T(2,128)(2,1)S(1)} %copy-done), kind=kOutput, calls=%fused_computation.20 | convolution fusion | flops 4294967296 | bytes 38273024 | tf_op jit(solution)/shard_map/dot_general | solution.py:22
  1191.9 16.5 %fusion.15 = f32[1024,8192]{1,0:T(8,128)} fusion(bf16[1,8192,256]{2,0,1:T(2,128)(2,1)} %get-tuple-element.29, bf16[1,256,1024]{2,0,1:T(2,128)(2,1)S(1)} %get-tuple-element.16), kind=kOutput, calls=%fused_computation.22 | convolution fusion | flops 4294967296 | bytes 38273024 | tf_op jit(solution)/shard_map/dot_general | solution.py:22
  1208.4 16.5 %fusion.9 = f32[1024,8192]{1,0:T(8,128)} fusion(bf16[1,8192,256]{2,0,1:T(2,128)(2,1)} %get-tuple-element.28, bf16[1,256,1024]{2,0,1:T(2,128)(2,1)S(1)} %get-tuple-element.16), kind=kOutput, calls=%fused_computation.16 | convolution fusion | flops 4294967296 | bytes 38273024 | tf_op jit(solution)/shard_map/dot_general | solution.py:22
  1225.0 16.5 %fusion.7 = f32[1024,8192]{1,0:T(8,128)} fusion(bf16[1,8192,256]{2,0,1:T(2,128)(2,1)} %get-tuple-element.20, bf16[1,256,1024]{2,0,1:T(2,128)(2,1)S(1)} %get-tuple-element.15), kind=kOutput, calls=%fused_computation.14 | convolution fusion | flops 4294967296 | bytes 38273024 | tf_op jit(solution)/shard_map/dot_general | solution.py:22
  1241.5 17.5 %fusion.3 = f32[1024,8192]{1,0:T(8,128)} fusion(bf16[1,8192,256]{2,0,1:T(2,128)(2,1)} %get-tuple-element.21, bf16[1,256,1024]{2,0,1:T(2,128)(2,1)S(1)} %get-tuple-element.15), kind=kOutput, calls=%fused_computation.10 | convolution fusion | flops 4294967296 | bytes 38273024 | tf_op jit(solution)/shard_map/dot_general | solution.py:22
  1259.0 40.7 %fusion.1 = bf16[1,1,1024,8192]{3,2,1,0:T(8,128)(2,1)} fusion(f32[1024,8192]{1,0:T(8,128)} %fusion.7, f32[1024,8192]{1,0:T(8,128)} %fusion.15, f32[1024,8192]{1,0:T(8,128)} %fusion.11, bf16[1,8192,256]{2,0,1:T(2,128)(2,1)} %get-tuple-element.21, bf16[1,256,1024]{2,0,1:T(2,128)(2,1)S(1)} %get-tuple-element.14), kind=kOutput, calls=%fused_computation.8 | convolution fusion | flops 4328521728 | bytes 122159104 | tf_op jit(solution)/shard_map/dot_general | solution.py:22
  1299.7 40.6 %fusion.2 = bf16[1,1,1024,8192]{3,2,1,0:T(8,128)(2,1)} fusion(f32[1024,8192]{1,0:T(8,128)} %fusion.3, f32[1024,8192]{1,0:T(8,128)} %fusion.9, f32[1024,8192]{1,0:T(8,128)} %fusion.13, bf16[1,8192,256]{2,0,1:T(2,128)(2,1)} %get-tuple-element.20, bf16[1,256,1024]{2,0,1:T(2,128)(2,1)S(1)} %get-tuple-element.14), kind=kOutput, calls=%fused_computation.9 | convolution fusion | flops 4328521728 | bytes 122159104 | tf_op jit(solution)/shard_map/dot_general | solution.py:22
  1340.3 23.0 %pad_maximum_fusion = bf16[1,2,1024,8192]{3,2,1,0:T(8,128)(2,1)} fusion(bf16[1,1,1024,8192]{3,2,1,0:T(8,128)(2,1)} %fusion.2, bf16[1,1,1024,8192]{3,2,1,0:T(8,128)(2,1)} %fusion.1), kind=kLoop, calls=%fused_computation.3 | loop fusion | flops 16777216 | bytes 67108864 | tf_op jit(solution)/shard_map/stack | solution.py:57
  (1 shorter events, 0.0 us)
Async XLA Ops:
  7.2 442.8 %all-gather.2.cloned.1.call-start = ((), (), s32[]{:S(2)}) async-start(), calls=%async_computation.1 | async-start | bytes 41943040 | tf_op jit(solution)/shard_map/all_gather | solution.py:39
  249.1 0.7 copy-start.1
  249.1 6.2 copy-start.2
  249.1 873.8 %all-reduce.3.cloned.1.call-start = ((), (), s32[]{:S(2)}) async-start(), calls=%async_computation.2 | async-start | bytes 33554432 | tf_op jit(solution)/shard_map/psum | solution.py:15
  1155.9 19.5 %copy-start = (bf16[1,256,1024]{2,0,1:T(2,128)(2,1)S(1)}, bf16[1,256,1024]{2,0,1:T(2,128)(2,1)}, u32[]{:S(2)}) copy-start(bf16[1,256,1024]{2,0,1:T(2,128)(2,1)} %get-tuple-element.17) | copy-start | bytes 1572868
Sparse Core Ops, SparseCore 0:
  249.2 200.6 all-gather.1
  612.5 510.3 all-reduce.2
where the time goes:
time: 1370 us
  waiting for transfers between devices  674 us (49%)
  matrix products  330 us (24%)
  blocking collectives  190 us (14%)
  local copies, waits for them, and re-layouts  115 us (8%)
  other arithmetic  40.3 us (3%)
  between operations  20.2 us (1%)
    psum x1, waiting for transfers between devices, spread(): return lax.psum(kept, axis)  480 us
    all_gather x1, waiting for transfers between devices, body(): gathered = lax.all_gather(by_row, 'freq', axis=1, tiled=True)  194 us
    all_to_all x1, blocking collectives, body(): lax.all_to_all(traces, 'row', split_axis=2, concat_axis=1, tiled=True)  190 us
    dot_general x8, matrix products, product(): lax.dot_general(first, second, dims, preferred_element_type=jnp.float32)  184 us
    dot_general x1, matrix products, body(): jnp.einsum('tsb,ct->csb', gathered, own_twiddle, preferred_element_type=j...  145 us
    unnamed x8, local copies, waits for them, and re-layouts  45 us
    slice x2, local copies, waits for them, and re-layouts, complex_terms(): real_part = product(left[0], right[0]) - product(left[1], right[1])  39.3 us
    all_to_all x1, local copies, waits for them, and re-layouts, body(): lax.all_to_all(traces, 'row', split_axis=2, concat_axis=1, tiled=True)  30.5 us
  transfers between devices with their start and end apart: 2, of which 2 were waited for; matrix products, arithmetic and copies ran while one was open for 2% of the time, Pallas kernels for 0%

commit v1 on v0

--- a/solution.py
+++ b/solution.py
@@ -36,7 +36,12 @@
     twiddle = jnp.stack([jnp.cos(angles), -jnp.sin(angles)], axis=1).astype(jnp.bfloat16)
     own_twiddle = lax.dynamic_index_in_dim(twiddle, lax.axis_index("freq"), 0, keepdims=False)
     by_row = lax.all_to_all(traces, "row", split_axis=2, concat_axis=1, tiled=True)
-    gathered = lax.all_gather(by_row, "freq", axis=1, tiled=True)
+    ring = [by_row]
+    for hop in range(3):
+        ring.append(lax.ppermute(ring[-1], "freq", [(dev, (dev + 1) % 4) for dev in range(4)]))
+    gathered = jnp.roll(
+        jnp.concatenate(ring[::-1], axis=1), (lax.axis_index("freq") + 1) * ring[0].shape[1], axis=1
+    )
     transformed = jnp.einsum(
         "tsb,ct->csb", gathered, own_twiddle, preferred_element_type=jnp.float32
     ).astype(jnp.bfloat16)

time: 1370 us -> 1520 us (1.11)
  waiting for transfers between devices: 674 us -> 752 us
  local copies, waits for them, and re-layouts: 115 us -> 178 us
    ppermute x0 -> x3, waiting for transfers between devices: none -> 273 us  [body(): lax.ppermute(ring[-1], 'freq', [(dev, (dev + 1) % 4) for dev in range(4)])]
    all_gather x1 -> x0, waiting for transfers between devices: 194 us -> none  [body(): gathered = lax.all_gather(by_row, 'freq', axis=1, tiled=True)]
    unnamed x8 -> x25, local copies, waits for them, and re-layouts: 45 us -> 101 us
  transfers between devices with their start and end apart: 2 -> 4, of which waited for: 2 -> 4; matrix products, arithmetic and copies ran while one was open for 2% -> 2% of each run, Pallas kernels for 0% -> 0%
where the time goes in v1:
time: 1520 us; the launch traced here: 1510 us
  waiting for transfers between devices  752 us (49%)
  matrix products  330 us (22%)
  blocking collectives  191 us (13%)
  local copies, waits for them, and re-layouts  178 us (12%)
  other arithmetic  40.3 us (3%)
  between operations  20.7 us (1%)
    psum x1, waiting for transfers between devices, spread(): return lax.psum(kept, axis)  479 us
    ppermute x3, waiting for transfers between devices, body(): lax.ppermute(ring[-1], 'freq', [(dev, (dev + 1) % 4) for dev in range(4)])  273 us
    all_to_all x1, blocking collectives, body(): lax.all_to_all(traces, 'row', split_axis=2, concat_axis=1, tiled=True)  191 us
    dot_general x8, matrix products, product(): lax.dot_general(first, second, dims, preferred_element_type=jnp.float32)  185 us
    dot_general x1, matrix products, body(): jnp.einsum('tsb,ct->csb', gathered, own_twiddle, preferred_element_type=j...  145 us
    unnamed x25, local copies, waits for them, and re-layouts  101 us
    slice x2, local copies, waits for them, and re-layouts, complex_terms(): real_part = product(left[0], right[0]) - product(left[1], right[1])  39.3 us
    all_to_all x1, local copies, waits for them, and re-layouts, body(): lax.all_to_all(traces, 'row', split_axis=2, concat_axis=1, tiled=True)  30.5 us
  transfers between devices with their start and end apart: 4, of which 4 were waited for; matrix products, arithmetic and copies ran while one was open for 2% of the time, Pallas kernels for 0%

profile of v1, /device:TPU:0, one launch (start us, length us, event | category | flops | bytes accessed | tf_op | source)
XLA Modules:
  0.0 1512.1 jit_solution(3943576727587876362)
XLA Ops:
  7.2 21.0 %copy.21 = bf16[2,256,8192]{1,0,2:T(2,128)(2,1)} copy(bf16[2,256,8192]{2,1,0:T(8,128)(2,1)} %param.4) | data formatting | bytes 16777216 | tf_op args[0]
  28.2 190.6 %all_to_all.18 = bf16[2,256,8192]{1,0,2:T(2,128)(2,1)} all-to-all(bf16[2,256,8192]{1,0,2:T(2,128)(2,1)} %copy.21), channel_id=1, replica_groups=mesh['freq'=4,'row'=8] {'row'}, dimensions={2} | all-to-all | bytes 16777216 | tf_op jit(solution)/shard_map/all_to_all | solution.py:38
  218.8 30.5 %copy.22 = bf16[2,256,8,1024]{3,0,1,2:T(2,128)(2,1)} copy(bf16[2,256,8,1024]{1,0,3,2:T(2,128)(2,1)} %bitcast.67) | data formatting | bytes 16777216 | tf_op jit(solution)/shard_map/all_to_all | solution.py:38
  249.3 93.1 %collective-permute-done = bf16[2,2048,1024]{2,0,1:T(2,128)(2,1)S(1)} collective-permute-done((bf16[2,2048,1024]{2,0,1:T(2,128)(2,1)}, bf16[2,2048,1024]{2,0,1:T(2,128)(2,1)S(1)}, u32[]{:S(2)}, u32[]{:S(2)}) %collective-permute-start) | collective-permute-done | bytes 8388640 | tf_op jit(solution)/shard_map/ppermute | solution.py:41
  342.3 3.4 copy-done
  345.7 93.0 %collective-permute-done.1 = bf16[2,2048,1024]{2,0,1:T(2,128)(2,1)} collective-permute-done((bf16[2,2048,1024]{2,0,1:T(2,128)(2,1)S(1)}, bf16[2,2048,1024]{2,0,1:T(2,128)(2,1)}, u32[]{:S(2)}, u32[]{:S(2)}) %collective-permute-start.1) | collective-permute-done | bytes 8388640 | tf_op jit(solution)/shard_map/ppermute | solution.py:41
  438.7 0.6 fusion.53
  444.5 0.2 fusion.49
  444.7 87.2 %collective-permute-done.2 = bf16[2,2048,1024]{2,0,1:T(2,128)(2,1)} collective-permute-done((bf16[2,2048,1024]{2,0,1:T(2,128)(2,1)}, bf16[2,2048,1024]{2,0,1:T(2,128)(2,1)}, u32[]{:S(2)}, u32[]{:S(2)}) %collective-permute-start.2) | collective-permute-done | bytes 8388640 | tf_op jit(solution)/shard_map/ppermute | solution.py:41
  531.9 8.0 constant_dynamic-update-slice_fusion.7
  539.9 8.1 constant_dynamic-update-slice_fusion.6
  548.1 7.0 constant_dynamic-update-slice_fusion.5
  555.1 7.0 constant_dynamic-update-slice_fusion.4
  562.2 8.0 constant_dynamic-update-slice_fusion.3
  570.2 8.0 constant_dynamic-update-slice_fusion.2
  578.2 7.0 constant_dynamic-update-slice_fusion.1
  585.2 6.9 constant_dynamic-update-slice_fusion
  592.1 145.4 %fusion = bf16[2,8192,1024]{2,0,1:T(2,128)(2,1)} fusion(bf16[1,2,8192,1024]{3,2,1,0:T(8,128)(2,1)} %param.5, bf16[2,16384,1024]{2,0,1:T(2,128)(2,1)} %constant_dynamic-update-slice_fusion, s32[]{:T(128)S(6)} %select_n.80, bf16[2,2]{1,0:T(2,128)(2,1)S(1)} %fusion.49), kind=kOutput, calls=%fused_computation.1 | convolution fusion | flops 150994944 | bytes 100663312 | tf_op jit(solution)/shard_map/tsb,ct->csb/dot_general | solution.py:45
  737.4 17.1 %broadcast_select_fusion.1 = (bf16[2,8192,256]{2,0,1:T(2,128)(2,1)}, bf16[2,8192,256]{2,0,1:T(2,128)(2,1)}) fusion(pred[]{:T(512)S(6)} %eq.14, bf16[2,8192,1024]{2,0,1:T(2,128)(2,1)} %fusion, s32[]{:T(128)S(6)} %select_n.85, s32[]{:T(128)S(6)} %select_n.91, pred[]{:T(512)S(6)} %eq.15), kind=kLoop, calls=%fused_computation.8 | loop fusion | flops 8388608 | bytes 33554440 | tf_op jit(solution)/shard_map/jit(_where)/select_n | solution.py:14
  755.8 23.4 %copy.23 = bf16[1,2,8192,1024]{3,2,1,0:T(8,128)(2,1)} copy(bf16[1,2,8192,1024]{3,1,2,0:T(2,128)(2,1)} %bitcast.59) | data formatting | bytes 67108864
  779.2 6.3 constant_dynamic-slice_fusion.3
  785.5 478.6 %all-reduce.3.cloned.1.call-done = (bf16[2,8192,256]{2,0,1:T(2,128)(2,1)}, bf16[2,8192,256]{2,0,1:T(2,128)(2,1)}) async-done(((bf16[2,8192,256]{2,0,1:T(2,128)(2,1)}, bf16[2,8192,256]{2,0,1:T(2,128)(2,1)}), (bf16[2,8192,256]{2,0,1:T(2,128)(2,1)}, bf16[2,8192,256]{2,0,1:T(2,128)(2,1)})) %all-reduce.3.cloned.1.call-update) | async-done | bytes 16777232 | tf_op jit(solution)/shard_map/psum | solution.py:15
  1264.2 33.0 %fusion.51 = (bf16[1,8192,256]{2,0,1:T(2,128)(2,1)}, bf16[1,8192,256]{2,0,1:T(2,128)(2,1)}, bf16[1,8192,256]{2,0,1:T(2,128)(2,1)}, bf16[1,8192,256]{2,0,1:T(2,128)(2,1)}) fusion(bf16[2,8192,256]{2,0,1:T(2,128)(2,1)} %get-tuple-element.12, bf16[2,8192,256]{2,0,1:T(2,128)(2,1)} %get-tuple-element.13), kind=kLoop, calls=%fused_computation.77 | loop fusion | bytes 33554432 | tf_op jit(solution)/shard_map/slice | solution.py:24
  1297.2 19.5 %fusion.14 = f32[1024,8192]{1,0:T(8,128)} fusion(bf16[1,8192,256]{2,0,1:T(2,128)(2,1)} %get-tuple-element.28, bf16[1,256,1024]{2,0,1:T(2,128)(2,1)} %get-tuple-element.17), kind=kOutput, calls=%fused_computation.19 | convolution fusion | flops 4294967296 | bytes 38273024 | tf_op jit(solution)/shard_map/dot_general | solution.py:22
  1316.7 16.7 %fusion.16 = f32[1024,8192]{1,0:T(8,128)} fusion(bf16[1,8192,256]{2,0,1:T(2,128)(2,1)} %get-tuple-element.29, bf16[1,256,1024]{2,0,1:T(2,128)(2,1)S(1)} %copy-done.1), kind=kOutput, calls=%fused_computation.21 | convolution fusion | flops 4294967296 | bytes 38273024 | tf_op jit(solution)/shard_map/dot_general | solution.py:22
  1333.4 16.5 %fusion.18 = f32[1024,8192]{1,0:T(8,128)} fusion(bf16[1,8192,256]{2,0,1:T(2,128)(2,1)} %get-tuple-element.29, bf16[1,256,1024]{2,0,1:T(2,128)(2,1)S(1)} %get-tuple-element.16), kind=kOutput, calls=%fused_computation.23 | convolution fusion | flops 4294967296 | bytes 38273024 | tf_op jit(solution)/shard_map/dot_general | solution.py:22
  1349.9 16.5 %fusion.12 = f32[1024,8192]{1,0:T(8,128)} fusion(bf16[1,8192,256]{2,0,1:T(2,128)(2,1)} %get-tuple-element.28, bf16[1,256,1024]{2,0,1:T(2,128)(2,1)S(1)} %get-tuple-element.16), kind=kOutput, calls=%fused_computation.17 | convolution fusion | flops 4294967296 | bytes 38273024 | tf_op jit(solution)/shard_map/dot_general | solution.py:22
  1366.5 16.6 %fusion.10 = f32[1024,8192]{1,0:T(8,128)} fusion(bf16[1,8192,256]{2,0,1:T(2,128)(2,1)} %get-tuple-element.20, bf16[1,256,1024]{2,0,1:T(2,128)(2,1)S(1)} %get-tuple-element.15), kind=kOutput, calls=%fused_computation.15 | convolution fusion | flops 4294967296 | bytes 38273024 | tf_op jit(solution)/shard_map/dot_general | solution.py:22
  1383.0 17.7 %fusion.6 = f32[1024,8192]{1,0:T(8,128)} fusion(bf16[1,8192,256]{2,0,1:T(2,128)(2,1)} %get-tuple-element.21, bf16[1,256,1024]{2,0,1:T(2,128)(2,1)S(1)} %get-tuple-element.15), kind=kOutput, calls=%fused_computation.11 | convolution fusion | flops 4294967296 | bytes 38273024 | tf_op jit(solution)/shard_map/dot_general | solution.py:22
  1400.7 40.7 %fusion.4 = bf16[1,1,1024,8192]{3,2,1,0:T(8,128)(2,1)} fusion(f32[1024,8192]{1,0:T(8,128)} %fusion.10, f32[1024,8192]{1,0:T(8,128)} %fusion.18, f32[1024,8192]{1,0:T(8,128)} %fusion.14, bf16[1,8192,256]{2,0,1:T(2,128)(2,1)} %get-tuple-element.21, bf16[1,256,1024]{2,0,1:T(2,128)(2,1)S(1)} %get-tuple-element.14), kind=kOutput, calls=%fused_computation.9 | convolution fusion | flops 4328521728 | bytes 122159104 | tf_op jit(solution)/shard_map/dot_general | solution.py:22
  1441.4 40.7 %fusion.5 = bf16[1,1,1024,8192]{3,2,1,0:T(8,128)(2,1)} fusion(f32[1024,8192]{1,0:T(8,128)} %fusion.6, f32[1024,8192]{1,0:T(8,128)} %fusion.12, f32[1024,8192]{1,0:T(8,128)} %fusion.16, bf16[1,8192,256]{2,0,1:T(2,128)(2,1)} %get-tuple-element.20, bf16[1,256,1024]{2,0,1:T(2,128)(2,1)S(1)} %get-tuple-element.14), kind=kOutput, calls=%fused_computation.10 | convolution fusion | flops 4328521728 | bytes 122159104 | tf_op jit(solution)/shard_map/dot_general | solution.py:22
  1482.1 23.0 %pad_maximum_fusion = bf16[1,2,1024,8192]{3,2,1,0:T(8,128)(2,1)} fusion(bf16[1,1,1024,8192]{3,2,1,0:T(8,128)(2,1)} %fusion.5, bf16[1,1,1024,8192]{3,2,1,0:T(8,128)(2,1)} %fusion.4), kind=kLoop, calls=%fused_computation.3 | loop fusion | flops 16777216 | bytes 67108864 | tf_op jit(solution)/shard_map/stack | solution.py:62
  (24 shorter events, 0.2 us)
Async XLA Ops:
  7.2 1257.0 %all-reduce.3.cloned.1.call-start = ((), (), s32[]{:S(2)}) async-start(), calls=%async_computation.1 | async-start | bytes 33554432 | tf_op jit(solution)/shard_map/psum | solution.py:15
  28.2 410.5 %copy-start.2 = (s32[2]{0:T(128)S(1)}, s32[2]{0:T(128)}, u32[]{:S(2)}) copy-start(s32[2]{0:T(128)} %param.7) | copy-start | bytes 28
  28.2 416.2 %copy-start.3 = (s32[4]{0:T(128)S(1)}, s32[4]{0:T(128)}, u32[]{:S(2)}) copy-start(s32[4]{0:T(128)} %param.6) | copy-start | bytes 52
  249.3 93.1 %collective-permute-start = (bf16[2,2048,1024]{2,0,1:T(2,128)(2,1)}, bf16[2,2048,1024]{2,0,1:T(2,128)(2,1)S(1)}, u32[]{:S(2)}, u32[]{:S(2)}) collective-permute-start(bf16[2,2048,1024]{2,0,1:T(2,128)(2,1)} %bitcast.60), channel_id=1, source_target_pairs={{0,8},{8,16},{16,24},{24,0},{1,9},{9,17},{17,25},{25,1},{2,10},{10... | collective-permute-start | bytes 25165832 | tf_op jit(solution)/shard_map/ppermute | solution.py:41
  342.3 3.4 copy-start
  345.7 93.0 %collective-permute-start.1 = (bf16[2,2048,1024]{2,0,1:T(2,128)(2,1)S(1)}, bf16[2,2048,1024]{2,0,1:T(2,128)(2,1)}, u32[]{:S(2)}, u32[]{:S(2)}) collective-permute-start(bf16[2,2048,1024]{2,0,1:T(2,128)(2,1)S(1)} %collective-permute-done), channel_id=1, source_target_pairs={{0,8},{8,16},{16,24},{24,0},{1,9},{9,17},{17,25},{25,1},{2,10},{10... | collective-permute-start | bytes 25165832 | tf_op jit(solution)/shard_map/ppermute | solution.py:41
  438.7 93.2 %collective-permute-start.2 = (bf16[2,2048,1024]{2,0,1:T(2,128)(2,1)}, bf16[2,2048,1024]{2,0,1:T(2,128)(2,1)}, u32[]{:S(2)}, u32[]{:S(2)}) collective-permute-start(bf16[2,2048,1024]{2,0,1:T(2,128)(2,1)} %collective-permute-done.1), channel_id=1, source_target_pairs={{0,8},{8,16},{16,24},{24,0},{1,9},{9,17},{17,25},{25,1},{2,10},{10... | collective-permute-start | bytes 25165832 | tf_op jit(solution)/shard_map/ppermute | solution.py:41
  444.5 103.5 %slice-start.2 = ((s8[8388608]{0:T(1024)(128)(4,1)}), s8[4194304]{0:T(1024)(128)(4,1)S(1)}, s32[]{:S(2)}) async-start(s8[8388608]{0:T(1024)(128)(4,1)} %bitcast.65), calls=%async_computation.4 | async-start | bytes 8388608
  444.7 103.4 %slice-start.3 = ((s8[8388608]{0:T(1024)(128)(4,1)}), s8[4194304]{0:T(1024)(128)(4,1)S(1)}, s32[]{:S(2)}) async-start(s8[8388608]{0:T(1024)(128)(4,1)} %bitcast.65), calls=%async_computation.5 | async-start | bytes 8388608
  539.9 15.2 %slice-start = ((s8[8388608]{0:T(1024)(128)(4,1)}), s8[4194304]{0:T(1024)(128)(4,1)S(1)}, s32[]{:S(2)}) async-start(s8[8388608]{0:T(1024)(128)(4,1)} %bitcast.61), calls=%async_computation.2 | async-start | bytes 8388608
  548.1 7.1 slice-start.1
  1297.2 19.5 %copy-start.1 = (bf16[1,256,1024]{2,0,1:T(2,128)(2,1)S(1)}, bf16[1,256,1024]{2,0,1:T(2,128)(2,1)}, u32[]{:S(2)}) copy-start(bf16[1,256,1024]{2,0,1:T(2,128)(2,1)} %get-tuple-element.17) | copy-start | bytes 1572868
Sparse Core Ops, SparseCore 0:
  754.7 509.4 all-reduce.2
